TPU v7x, 512 devices: a whole 4x4x16 slice. The times are simulated.
512 devices in a mesh: seq: 128 (over x, z, y_hi), batch: 4 (over y_lo, core).
Axes of the slice: x: 4, y: 4 (y_hi: 2, y_lo: 2; y = y_hi * 2 + y_lo), z: 16, core: 2. Of those that a mesh axis runs over, the one named last changes fastest.
Arguments:
- inputs: bfloat16 [4, 128, 16384], P('batch', None, 'seq'), may hold values from -6 to 6
- out_grad: bfloat16 [4, 128, 16384], P('batch', None, 'seq'), may hold values from -0.046875 to 0.046875
- filters: float32 [128, 16384], P(None, 'seq'), may hold values from -6 to 6
Outputs:
- in_grad: bfloat16 [4, 128, 16384], P('batch', None, 'seq')
- filter_grad: float32 [128, 16384], P(None, 'seq')
All inputs are finite; a program needn't handle non-finite values.
Results may differ from a plain program's by a relative error of at most 0.0025.
Values sent between devices are 32-bit elements; how exact they have to be, the bound alone decides.
No kernel may reach another device: no remote copies, remote signals or barrier semaphores. Data moves between devices by JAX's collectives and lax.ppermute only.
A program may use at most 64 MiB of HBM per device.

v0:
```python
import math
import jax
import jax.numpy as jnp
from jax import lax
from jax.sharding import PartitionSpec as P

FACTOR = 16


def contract(pattern, operand, weights):
    return jnp.einsum(
        pattern,
        operand,
        weights,
        precision=lax.Precision.HIGHEST,
        preferred_element_type=jnp.float32,
    )


def angles(left_index, right_index, modulus):
    product = left_index[:, None] * right_index[None, :] % modulus
    return product.astype(jnp.float32) * (2.0 * math.pi / modulus)


def rotate(pattern, real_part, imag_part, angle_table, orient):
    cosine = jnp.cos(angle_table)
    sine_part = jnp.sin(angle_table)
    new_real = contract(pattern, real_part, cosine) - orient * contract(
        pattern, imag_part, sine_part
    )
    new_imag = contract(pattern, imag_part, cosine) + orient * contract(
        pattern, real_part, sine_part
    )
    return (new_real, new_imag)


def twist(real_part, imag_part, angle_table, orient):
    cosine = jnp.cos(angle_table)
    sine_part = jnp.sin(angle_table)
    return (
        real_part * cosine - orient * imag_part * sine_part,
        imag_part * cosine + orient * real_part * sine_part,
    )


def local_tables(length_all):
    inner = length_all // FACTOR
    outer_index = jnp.arange(FACTOR, dtype=jnp.int32)
    inner_index = jnp.arange(inner, dtype=jnp.int32)
    outer_table = angles(outer_index, outer_index, FACTOR)
    mid_table = angles(outer_index, inner_index, length_all)
    inner_table = angles(inner_index, inner_index, inner)
    return (outer_table, mid_table, inner_table)


def local_forward(real_part, imag_part):
    row_count, held, length_all = real_part.shape
    outer_table, mid_table, inner_table = local_tables(length_all)
    real_part = real_part.reshape(row_count, held, FACTOR, length_all // FACTOR)
    imag_part = imag_part.reshape(row_count, held, FACTOR, length_all // FACTOR)
    real_part, imag_part = rotate("kiuv,uq->kiqv", real_part, imag_part, outer_table, -1.0)
    real_part, imag_part = twist(real_part, imag_part, mid_table, -1.0)
    return rotate("kiqv,vm->kiqm", real_part, imag_part, inner_table, -1.0)


def local_inverse(real_part, imag_part):
    row_count, held, outer, inner = real_part.shape
    outer_table, mid_table, inner_table = local_tables(outer * inner)
    real_part, imag_part = rotate("kiqm,mv->kiqv", real_part, imag_part, inner_table, 1.0)
    real_part, imag_part = twist(real_part, imag_part, mid_table, 1.0)
    real_part, imag_part = rotate("kiqv,qu->kiuv", real_part, imag_part, outer_table, 1.0)
    return (
        real_part.reshape(row_count, held, outer * inner),
        imag_part.reshape(row_count, held, outer * inner),
    )


def body(inputs, out_grad, filters):
    seq_count = lax.axis_size("seq")
    position = lax.axis_index("seq")
    length_dev = inputs.shape[2]
    block_len = length_dev // seq_count
    total_len = 2 * seq_count * length_dev
    channels = inputs.shape[1]
    stacked = jnp.concatenate(
        [inputs[0].astype(jnp.float32), out_grad[0].astype(jnp.float32), filters], axis=0
    )
    row_count = stacked.shape[0]
    spread = lax.all_to_all(
        stacked.reshape(row_count, seq_count, block_len),
        "seq",
        split_axis=1,
        concat_axis=1,
        tiled=True,
    )
    low_index = jnp.arange(seq_count, dtype=jnp.int32)
    second_freq = jnp.where(low_index == 0, seq_count, 2 * seq_count - low_index)
    freq_order = jnp.stack([low_index, second_freq], axis=1).reshape(2 * seq_count)
    cross_table = angles(low_index, freq_order, 2 * seq_count)
    local_cols = position * block_len + jnp.arange(block_len, dtype=jnp.int32)
    cols_twist = angles(freq_order, local_cols, total_len)
    real_part = contract("kaj,am->kmj", spread, jnp.cos(cross_table))
    imag_part = -contract("kaj,am->kmj", spread, jnp.sin(cross_table))
    real_part, imag_part = twist(real_part, imag_part, cols_twist, -1.0)
    cols_real, cols_imag = (
        lax.all_to_all(real_part, "seq", split_axis=1, concat_axis=2, tiled=True),
        lax.all_to_all(imag_part, "seq", split_axis=1, concat_axis=2, tiled=True),
    )
    spec_real, spec_imag = local_forward(cols_real, cols_imag)
    input_real = spec_real[:channels]
    input_imag = spec_imag[:channels]
    grad_real = spec_real[channels : 2 * channels]
    grad_imag = spec_imag[channels : 2 * channels]
    filter_real = spec_real[2 * channels :]
    filter_imag = spec_imag[2 * channels :]
    first_real = filter_real * grad_real + filter_imag * grad_imag
    first_imag = filter_real * grad_imag - filter_imag * grad_real
    second_real = input_real * grad_real + input_imag * grad_imag
    second_imag = input_real * grad_imag - input_imag * grad_real
    joined_real = jnp.concatenate([first_real, second_real], axis=0)
    joined_imag = jnp.concatenate([first_imag, second_imag], axis=0)
    held_freq = lax.dynamic_slice_in_dim(freq_order, 2 * position, 2)
    all_cols = jnp.arange(length_dev, dtype=jnp.int32)
    back_twist = angles(held_freq, all_cols, total_len)
    back_table = angles(freq_order, low_index, 2 * seq_count)
    factor_scale = 1.0 / total_len
    cos_back = jnp.cos(back_table) * factor_scale
    sin_back = jnp.sin(back_table) * factor_scale
    back_real, back_imag = local_inverse(joined_real, joined_imag)
    back_real, back_imag = twist(back_real, back_imag, back_twist, 1.0)
    gath_real, gath_imag = (
        lax.all_to_all(back_real, "seq", split_axis=2, concat_axis=1, tiled=True),
        lax.all_to_all(back_imag, "seq", split_axis=2, concat_axis=1, tiled=True),
    )
    rebuilt = contract("kmj,ma->kaj", gath_real, cos_back) - contract(
        "kmj,ma->kaj", gath_imag, sin_back
    )
    returned = lax.all_to_all(rebuilt, "seq", split_axis=1, concat_axis=2, tiled=True)[:, 0, :]
    in_grad = returned[:channels].astype(jnp.bfloat16)[None]
    partial_grad = returned[channels:]
    filter_grad = lax.psum(partial_grad, "batch")
    return (in_grad, filter_grad)


def solution(mesh):
    placed = (P("batch", None, "seq"), P("batch", None, "seq"), P(None, "seq"))
    return jax.shard_map(
        body,
        mesh=mesh,
        in_specs=placed,
        out_specs=(P("batch", None, "seq"), P(None, "seq")),
        check_vma=False,
    )
```

profile of v0, /device:TPU:1, one launch (start us, length us, event | category | flops | bytes accessed | tf_op | source)
XLA Modules:
  0.0 269.2 jit_solution(8236200142034256242)
XLA Ops:
  7.2 0.9 copy.67
  8.4 0.8 reshape.208
  9.2 23.0 %all-to-all-start = ((f32[384,128,1]{0,2,1:T(1,128)}), f32[384,128,1]{0,2,1:T(1,128)S(1)}, u32[]{:S(2)}, u32[]{:S(2)}) async-start(f32[384,128,1]{0,2,1:T(1,128)} %reshape.208), calls=%async_computation | async-start | bytes 393216 | tf_op jit(solution)/shard_map/all_to_all | solution.py:89
  32.3 0.1 mul.547
  32.5 19.3 %all-to-all-done = f32[384,128,1]{0,2,1:T(1,128)S(1)} async-done(((f32[384,128,1]{0,2,1:T(1,128)}), f32[384,128,1]{0,2,1:T(1,128)S(1)}, u32[]{:S(2)}, u32[]{:S(2)}) %all-to-all-start) | async-done | bytes 196640 | tf_op jit(solution)/shard_map/all_to_all | solution.py:89
  51.8 1.0 fusion
  52.8 1.0 add_bitcast_fusion.1
  53.8 1.2 copy.70
  55.0 7.5 %all-to-all-start.1 = ((f32[384,256,1]{0,2,1:T(1,128)}), f32[384,256,1]{0,2,1:T(1,128)S(1)}, u32[]{:S(2)}, u32[]{:S(2)}) async-start(f32[384,256,1]{0,2,1:T(1,128)} %copy.70), calls=%async_computation.1 | async-start | bytes 786432 | tf_op jit(solution)/shard_map/all_to_all | solution.py:106
  62.5 1.1 copy.73
  63.6 23.8 %all-to-all-done.1 = f32[384,256,1]{0,2,1:T(1,128)S(1)} async-done(((f32[384,256,1]{0,2,1:T(1,128)}), f32[384,256,1]{0,2,1:T(1,128)S(1)}, u32[]{:S(2)}, u32[]{:S(2)}) %all-to-all-start.1) | async-done | bytes 393248 | tf_op jit(solution)/shard_map/all_to_all | solution.py:106
  87.4 10.3 %all-to-all-start.2 = ((f32[384,256,1]{0,2,1:T(1,128)}), f32[384,256,1]{0,2,1:T(1,128)S(1)}, u32[]{:S(2)}, u32[]{:S(2)}) async-start(f32[384,256,1]{0,2,1:T(1,128)} %copy.73), calls=%async_computation.2 | async-start | bytes 786432 | tf_op jit(solution)/shard_map/all_to_all | solution.py:107
  98.0 0.1 fusion.114
  98.2 0.5 convolution_multiply_fusion.2
  98.7 23.6 %all-to-all-done.2 = f32[384,256,1]{0,2,1:T(1,128)S(1)} async-done(((f32[384,256,1]{0,2,1:T(1,128)}), f32[384,256,1]{0,2,1:T(1,128)S(1)}, u32[]{:S(2)}, u32[]{:S(2)}) %all-to-all-start.2) | async-done | bytes 393248 | tf_op jit(solution)/shard_map/all_to_all | solution.py:107
  122.3 0.5 convolution_multiply_fusion.3
  122.9 0.5 convolution_add_fusion.1
  123.4 0.6 add_bitcast_fusion
  124.0 0.6 convolution_multiply_fusion.1
  124.6 0.6 convolution_multiply_fusion
  125.2 0.6 convolution_subtract_fusion
  125.8 0.6 convolution_add_fusion
  126.4 0.4 fusion.20
  126.8 0.4 fusion.21
  127.2 0.4 convolution_subtract_fusion.3
  127.6 0.5 multiply_subtract_fusion
  128.1 0.4 fusion.18
  128.5 0.4 fusion.14
  129.0 0.4 fusion.2
  129.4 0.4 fusion.1
  129.8 0.3 fusion.13
  130.1 0.9 copy.90
  131.0 10.1 %all-to-all-start.3 = ((f32[256,2,128]{0,1,2:T(2,128)}), f32[256,2,128]{0,1,2:T(2,128)S(1)}, u32[]{:S(2)}, u32[]{:S(2)}) async-start(f32[256,2,128]{0,1,2:T(2,128)} %copy.90), calls=%async_computation.3 | async-start | bytes 524288 | tf_op jit(solution)/shard_map/all_to_all | solution.py:132
  141.2 0.9 copy.91
  142.1 19.4 %all-to-all-done.3 = f32[256,2,128]{0,1,2:T(2,128)S(1)} async-done(((f32[256,2,128]{0,1,2:T(2,128)}), f32[256,2,128]{0,1,2:T(2,128)S(1)}, u32[]{:S(2)}, u32[]{:S(2)}) %all-to-all-start.3) | async-done | bytes 262176 | tf_op jit(solution)/shard_map/all_to_all | solution.py:132
  161.4 9.2 %all-to-all-start.4 = ((f32[256,2,128]{0,1,2:T(2,128)}), f32[256,2,128]{0,1,2:T(2,128)S(1)}, u32[]{:S(2)}, u32[]{:S(2)}) async-start(f32[256,2,128]{0,1,2:T(2,128)} %copy.91), calls=%async_computation.4 | async-start | bytes 524288 | tf_op jit(solution)/shard_map/all_to_all | solution.py:133
  170.7 0.3 all-reduce.2.cloned.1.call-start
  170.9 0.2 reshape.214
  171.1 0.9 fusion.38
  172.1 19.0 %all-to-all-done.4 = f32[256,2,128]{0,1,2:T(2,128)S(1)} async-done(((f32[256,2,128]{0,1,2:T(2,128)}), f32[256,2,128]{0,1,2:T(2,128)S(1)}, u32[]{:S(2)}, u32[]{:S(2)}) %all-to-all-start.4) | async-done | bytes 262176 | tf_op jit(solution)/shard_map/all_to_all | solution.py:133
  191.1 0.2 reshape.215
  191.2 0.9 fusion.3
  192.2 0.1 copy.92
  192.3 25.7 %all_to_all.74 = f32[256,128,1]{0,2,1:T(1,128)S(1)} all-to-all(f32[256,128,1]{0,2,1:T(1,128)S(1)} %copy.92), channel_id=1, replica_groups=mesh['seq'=128,'batch'=4] {'seq'}, dimensions={1} | all-to-all | bytes 262144 | tf_op jit(solution)/shard_map/all_to_all | solution.py:138
  218.0 0.7 slice.46
  218.8 0.7 copy.100
  219.5 41.3 %all-reduce.2.cloned.1.call-done = f32[128,128]{0,1:T(8,128)} async-done(((f32[128,128]{0,1:T(8,128)}), f32[128,128]{0,1:T(8,128)}) %all-reduce.2.cloned.1.call-update) | async-done | bytes 65552 | tf_op jit(solution)/shard_map/psum | solution.py:141
  260.8 1.6 copy.94
  (24 shorter events, 1.0 us)
Async XLA Ops:
  7.2 0.9 copy-start.1
  7.2 1.0 copy-start
  9.2 42.6 %all-to-all-start = ((f32[384,128,1]{0,2,1:T(1,128)}), f32[384,128,1]{0,2,1:T(1,128)S(1)}, u32[]{:S(2)}, u32[]{:S(2)}) async-start(f32[384,128,1]{0,2,1:T(1,128)} %reshape.208), calls=%async_computation | async-start | bytes 393216 | tf_op jit(solution)/shard_map/all_to_all | solution.py:89
  55.0 32.4 %all-to-all-start.1 = ((f32[384,256,1]{0,2,1:T(1,128)}), f32[384,256,1]{0,2,1:T(1,128)S(1)}, u32[]{:S(2)}, u32[]{:S(2)}) async-start(f32[384,256,1]{0,2,1:T(1,128)} %copy.70), calls=%async_computation.1 | async-start | bytes 786432 | tf_op jit(solution)/shard_map/all_to_all | solution.py:106
  87.4 34.9 %all-to-all-start.2 = ((f32[384,256,1]{0,2,1:T(1,128)}), f32[384,256,1]{0,2,1:T(1,128)S(1)}, u32[]{:S(2)}, u32[]{:S(2)}) async-start(f32[384,256,1]{0,2,1:T(1,128)} %copy.73), calls=%async_computation.2 | async-start | bytes 786432 | tf_op jit(solution)/shard_map/all_to_all | solution.py:107
  131.0 30.4 %all-to-all-start.3 = ((f32[256,2,128]{0,1,2:T(2,128)}), f32[256,2,128]{0,1,2:T(2,128)S(1)}, u32[]{:S(2)}, u32[]{:S(2)}) async-start(f32[256,2,128]{0,1,2:T(2,128)} %copy.90), calls=%async_computation.3 | async-start | bytes 524288 | tf_op jit(solution)/shard_map/all_to_all | solution.py:132
  161.4 29.6 %all-to-all-start.4 = ((f32[256,2,128]{0,1,2:T(2,128)}), f32[256,2,128]{0,1,2:T(2,128)S(1)}, u32[]{:S(2)}, u32[]{:S(2)}) async-start(f32[256,2,128]{0,1,2:T(2,128)} %copy.91), calls=%async_computation.4 | async-start | bytes 524288 | tf_op jit(solution)/shard_map/all_to_all | solution.py:133
  170.7 90.1 %all-reduce.2.cloned.1.call-start = ((), (), s32[]{:S(2)}) async-start(), calls=%async_computation.6 | async-start | bytes 131072 | tf_op jit(solution)/shard_map/psum | solution.py:141
Sparse Core Ops, SparseCore 0:
  218.9 41.8 all-reduce.1
where the time goes:
time: 270 us; the launch traced here: 269 us
  waiting for transfers between devices  146 us (54%)
  starting transfers between devices  60.3 us (22%)
  blocking collectives  25.7 us (10%)
  between operations  14.4 us (5%)
  matrix products  11.7 us (4%)
  local copies, waits for them, and re-layouts  10 us (4%)
    psum x1, waiting for transfers between devices, body(): filter_grad = lax.psum(partial_grad, 'batch')  41.3 us
    all_to_all x1, blocking collectives, body(): lax.all_to_all(rebuilt, 'seq', split_axis=1, concat_axis=2, tiled=True)  25.7 us
    all_to_all x1, waiting for transfers between devices, body(): lax.all_to_all(real_part, 'seq', split_axis=1, concat_axis=2, tiled=True)  23.8 us
    all_to_all x1, waiting for transfers between devices, body(): lax.all_to_all(imag_part, 'seq', split_axis=1, concat_axis=2, tiled=True)  23.6 us
    all_to_all x1, starting transfers between devices, body(): lax.all_to_all(stacked.reshape(row_count, seq_count, block_len), 'seq', s...  23 us
    all_to_all x1, waiting for transfers between devices, body(): lax.all_to_all(back_real, 'seq', split_axis=2, concat_axis=1, tiled=True)  19.4 us
    all_to_all x1, waiting for transfers between devices, body(): lax.all_to_all(stacked.reshape(row_count, seq_count, block_len), 'seq', s...  19.3 us
    all_to_all x1, waiting for transfers between devices, body(): lax.all_to_all(back_imag, 'seq', split_axis=2, concat_axis=1, tiled=True)  19 us
  transfers between devices with their start and end apart: 6, of which 6 were waited for; matrix products, arithmetic and copies ran while one was open for 2% of the time, Pallas kernels for 0%

commit v1 on v0

--- a/solution.py
+++ b/solution.py
@@ -138,7 +138,8 @@
     returned = lax.all_to_all(rebuilt, "seq", split_axis=1, concat_axis=2, tiled=True)[:, 0, :]
     in_grad = returned[:channels].astype(jnp.bfloat16)[None]
     partial_grad = returned[channels:]
-    filter_grad = lax.psum(partial_grad, "batch")
+    pieces = lax.all_gather(partial_grad, "batch", axis=0, tiled=False)
+    filter_grad = pieces.sum(axis=0)
     return (in_grad, filter_grad)
 
 

time: 270 us -> 223 us (0.83)
  waiting for transfers between devices: 146 us -> 105 us
  between operations: 14.4 us -> 1 us
  blocking collectives: 25.7 us -> 35 us
    psum x1 -> x0, waiting for transfers between devices: 41.3 us -> none  [body(): filter_grad = lax.psum(partial_grad, 'batch')]
    all_gather x0 -> x1, blocking collectives: none -> 9.28 us  [body(): pieces = lax.all_gather(partial_grad, 'batch', axis=0, tiled=False)]
  transfers between devices with their start and end apart: 6 -> 5, of which waited for: 6 -> 5; matrix products, arithmetic and copies ran while one was open for 2% -> 2% of each run, Pallas kernels for 0% -> 0%
where the time goes in v1:
time: 223 us
  waiting for transfers between devices  105 us (47%)
  starting transfers between devices  59.9 us (27%)
  blocking collectives  35 us (16%)
  matrix products  11.7 us (5%)
  local copies, waits for them, and re-layouts  8.62 us (4%)
    all_to_all x1, blocking collectives, body(): lax.all_to_all(rebuilt, 'seq', split_axis=1, concat_axis=2, tiled=True)  25.7 us
    all_to_all x1, waiting for transfers between devices, body(): lax.all_to_all(real_part, 'seq', split_axis=1, concat_axis=2, tiled=True)  23.8 us
    all_to_all x1, waiting for transfers between devices, body(): lax.all_to_all(imag_part, 'seq', split_axis=1, concat_axis=2, tiled=True)  23.6 us
    all_to_all x1, starting transfers between devices, body(): lax.all_to_all(stacked.reshape(row_count, seq_count, block_len), 'seq', s...  23 us
    all_to_all x1, waiting for transfers between devices, body(): lax.all_to_all(back_real, 'seq', split_axis=2, concat_axis=1, tiled=True)  19.6 us
    all_to_all x1, waiting for transfers between devices, body(): lax.all_to_all(stacked.reshape(row_count, seq_count, block_len), 'seq', s...  19.3 us
    all_to_all x1, waiting for transfers between devices, body(): lax.all_to_all(back_imag, 'seq', split_axis=2, concat_axis=1, tiled=True)  19 us
    dot_general x20, matrix products, contract(): jnp.einsum(pattern, operand, weights, precision=lax.Precision.HIGHEST, pr...  11.7 us
  transfers between devices with their start and end apart: 5, of which 5 were waited for; matrix products, arithmetic and copies ran while one was open for 2% of the time, Pallas kernels for 0%

profile of v1, /device:TPU:1, one launch (start us, length us, event | category | flops | bytes accessed | tf_op | source)
XLA Modules:
  0.0 222.5 jit_solution(988739216877438854)
XLA Ops:
  0.6 0.9 copy.65
  1.6 0.1 copy.66
  1.8 0.8 reshape.209
  2.7 23.0 %all-to-all-start = ((f32[384,128,1]{0,2,1:T(1,128)}), f32[384,128,1]{0,2,1:T(1,128)S(1)}, u32[]{:S(2)}, u32[]{:S(2)}) async-start(f32[384,128,1]{0,2,1:T(1,128)} %reshape.209), calls=%async_computation | async-start | bytes 393216 | tf_op jit(solution)/shard_map/all_to_all | solution.py:89
  25.8 0.1 mul.547
  26.0 19.3 %all-to-all-done = f32[384,128,1]{0,2,1:T(1,128)S(1)} async-done(((f32[384,128,1]{0,2,1:T(1,128)}), f32[384,128,1]{0,2,1:T(1,128)S(1)}, u32[]{:S(2)}, u32[]{:S(2)}) %all-to-all-start) | async-done | bytes 196640 | tf_op jit(solution)/shard_map/all_to_all | solution.py:89
  45.3 1.0 fusion
  46.3 1.0 add_bitcast_fusion.1
  47.3 1.2 copy.68
  48.5 7.5 %all-to-all-start.1 = ((f32[384,256,1]{0,2,1:T(1,128)}), f32[384,256,1]{0,2,1:T(1,128)S(1)}, u32[]{:S(2)}, u32[]{:S(2)}) async-start(f32[384,256,1]{0,2,1:T(1,128)} %copy.68), calls=%async_computation.1 | async-start | bytes 786432 | tf_op jit(solution)/shard_map/all_to_all | solution.py:106
  55.9 1.1 copy.71
  57.1 23.8 %all-to-all-done.1 = f32[384,256,1]{0,2,1:T(1,128)S(1)} async-done(((f32[384,256,1]{0,2,1:T(1,128)}), f32[384,256,1]{0,2,1:T(1,128)S(1)}, u32[]{:S(2)}, u32[]{:S(2)}) %all-to-all-start.1) | async-done | bytes 393248 | tf_op jit(solution)/shard_map/all_to_all | solution.py:106
  80.9 10.2 %all-to-all-start.2 = ((f32[384,256,1]{0,2,1:T(1,128)}), f32[384,256,1]{0,2,1:T(1,128)S(1)}, u32[]{:S(2)}, u32[]{:S(2)}) async-start(f32[384,256,1]{0,2,1:T(1,128)} %copy.71), calls=%async_computation.2 | async-start | bytes 786432 | tf_op jit(solution)/shard_map/all_to_all | solution.py:107
  91.5 0.1 fusion.114
  91.6 0.5 convolution_multiply_fusion.2
  92.2 23.6 %all-to-all-done.2 = f32[384,256,1]{0,2,1:T(1,128)S(1)} async-done(((f32[384,256,1]{0,2,1:T(1,128)}), f32[384,256,1]{0,2,1:T(1,128)S(1)}, u32[]{:S(2)}, u32[]{:S(2)}) %all-to-all-start.2) | async-done | bytes 393248 | tf_op jit(solution)/shard_map/all_to_all | solution.py:107
  115.8 0.5 convolution_multiply_fusion.3
  116.4 0.5 convolution_add_fusion.1
  116.9 0.6 add_bitcast_fusion
  117.5 0.6 convolution_multiply_fusion.1
  118.1 0.6 convolution_multiply_fusion
  118.7 0.6 convolution_subtract_fusion
  119.3 0.6 convolution_add_fusion
  119.9 0.4 fusion.20
  120.3 0.4 fusion.21
  120.7 0.4 convolution_subtract_fusion.3
  121.1 0.5 multiply_subtract_fusion
  121.6 0.4 fusion.18
  122.0 0.4 fusion.14
  122.5 0.4 fusion.2
  122.9 0.4 fusion.1
  123.3 0.3 fusion.13
  123.6 0.9 copy.88
  124.5 10.1 %all-to-all-start.3 = ((f32[256,2,128]{0,1,2:T(2,128)}), f32[256,2,128]{0,1,2:T(2,128)S(1)}, u32[]{:S(2)}, u32[]{:S(2)}) async-start(f32[256,2,128]{0,1,2:T(2,128)} %copy.88), calls=%async_computation.3 | async-start | bytes 524288 | tf_op jit(solution)/shard_map/all_to_all | solution.py:132
  134.6 0.9 copy.89
  135.5 19.6 %all-to-all-done.3 = f32[256,2,128]{0,1,2:T(2,128)S(1)} async-done(((f32[256,2,128]{0,1,2:T(2,128)}), f32[256,2,128]{0,1,2:T(2,128)S(1)}, u32[]{:S(2)}, u32[]{:S(2)}) %all-to-all-start.3) | async-done | bytes 262176 | tf_op jit(solution)/shard_map/all_to_all | solution.py:132
  155.1 9.2 %all-to-all-start.4 = ((f32[256,2,128]{0,1,2:T(2,128)}), f32[256,2,128]{0,1,2:T(2,128)S(1)}, u32[]{:S(2)}, u32[]{:S(2)}) async-start(f32[256,2,128]{0,1,2:T(2,128)} %copy.89), calls=%async_computation.4 | async-start | bytes 524288 | tf_op jit(solution)/shard_map/all_to_all | solution.py:133
  164.4 0.2 reshape.215
  164.5 0.9 fusion.38
  165.5 19.0 %all-to-all-done.4 = f32[256,2,128]{0,1,2:T(2,128)S(1)} async-done(((f32[256,2,128]{0,1,2:T(2,128)}), f32[256,2,128]{0,1,2:T(2,128)S(1)}, u32[]{:S(2)}, u32[]{:S(2)}) %all-to-all-start.4) | async-done | bytes 262176 | tf_op jit(solution)/shard_map/all_to_all | solution.py:133
  184.5 0.2 reshape.216
  184.7 0.9 fusion.3
  185.7 0.1 copy.90
  185.8 25.7 %all_to_all.74 = f32[256,128,1]{0,2,1:T(1,128)S(1)} all-to-all(f32[256,128,1]{0,2,1:T(1,128)S(1)} %copy.90), channel_id=1, replica_groups=mesh['seq'=128,'batch'=4] {'seq'}, dimensions={1} | all-to-all | bytes 262144 | tf_op jit(solution)/shard_map/all_to_all | solution.py:138
  211.6 9.3 %all-gather = f32[512,128,1]{0,2,1:T(1,128)S(1)} all-gather(f32[128,128,1]{0,2,1:T(1,128)S(1)} %slice.43), channel_id=2, replica_groups=mesh['seq'=128,'batch'=4] {'batch'}, dimensions={0}, use_global_device_ids=true | all-gather | bytes 327680 | tf_op jit(solution)/shard_map/all_gather | solution.py:141
  220.8 0.2 reduce_sum.9
  221.0 0.7 copy.92
  221.8 0.7 copy.98
  (23 shorter events, 0.9 us)
Async XLA Ops:
  0.6 0.9 copy-start.1
  0.6 1.0 copy-start
  2.7 42.6 %all-to-all-start = ((f32[384,128,1]{0,2,1:T(1,128)}), f32[384,128,1]{0,2,1:T(1,128)S(1)}, u32[]{:S(2)}, u32[]{:S(2)}) async-start(f32[384,128,1]{0,2,1:T(1,128)} %reshape.209), calls=%async_computation | async-start | bytes 393216 | tf_op jit(solution)/shard_map/all_to_all | solution.py:89
  48.5 32.4 %all-to-all-start.1 = ((f32[384,256,1]{0,2,1:T(1,128)}), f32[384,256,1]{0,2,1:T(1,128)S(1)}, u32[]{:S(2)}, u32[]{:S(2)}) async-start(f32[384,256,1]{0,2,1:T(1,128)} %copy.68), calls=%async_computation.1 | async-start | bytes 786432 | tf_op jit(solution)/shard_map/all_to_all | solution.py:106
  80.9 34.9 %all-to-all-start.2 = ((f32[384,256,1]{0,2,1:T(1,128)}), f32[384,256,1]{0,2,1:T(1,128)S(1)}, u32[]{:S(2)}, u32[]{:S(2)}) async-start(f32[384,256,1]{0,2,1:T(1,128)} %copy.71), calls=%async_computation.2 | async-start | bytes 786432 | tf_op jit(solution)/shard_map/all_to_all | solution.py:107
  124.5 30.6 %all-to-all-start.3 = ((f32[256,2,128]{0,1,2:T(2,128)}), f32[256,2,128]{0,1,2:T(2,128)S(1)}, u32[]{:S(2)}, u32[]{:S(2)}) async-start(f32[256,2,128]{0,1,2:T(2,128)} %copy.88), calls=%async_computation.3 | async-start | bytes 524288 | tf_op jit(solution)/shard_map/all_to_all | solution.py:132
  155.1 29.4 %all-to-all-start.4 = ((f32[256,2,128]{0,1,2:T(2,128)}), f32[256,2,128]{0,1,2:T(2,128)S(1)}, u32[]{:S(2)}, u32[]{:S(2)}) async-start(f32[256,2,128]{0,1,2:T(2,128)} %copy.89), calls=%async_computation.4 | async-start | bytes 524288 | tf_op jit(solution)/shard_map/all_to_all | solution.py:133
